TPU v7x, 512 devices: a whole 4x8x8 slice. The times are simulated.
512 devices in a mesh: section: 4 (over z_hi, core), seq: 32 (over x, y), head: 4 (over z_lo).
Axes of the slice: x: 4, y: 8, z: 8 (z_hi: 2, z_lo: 4; z = z_hi * 4 + z_lo), core: 2. Of those that a mesh axis runs over, the one named last changes fastest.
Arguments:
- query_heads: bfloat16 [4, 6144, 3072], P('section', 'seq', 'head'), may hold values from -6 to 6
- key_heads: bfloat16 [4, 6144, 3072], P('section', 'seq', 'head'), may hold values from -6 to 6
- value_heads: bfloat16 [4, 6144, 3072], P('section', 'seq', 'head'), may hold values from -6 to 6
- stream: bfloat16 [4, 6144, 3072], P('section', 'seq', 'head'), may hold values from -1.5 to 1.5
- out_weight: bfloat16 [4, 3072, 3072], P('section', 'head', 'seq'), may hold values from -0.109375 to 0.109375
- gate_scale: float32 [4, 3072], P('section', 'head'), may hold values from 0.5 to 1.5
- windows: int32 [16, 27], replicated, may hold values from -1 to 15, as said below
Outputs:
- handed: bfloat16 [4, 6144, 3072], P('section', 'seq', 'head')
Inputs may be any that keep to these rules, and one draw needn't show every extreme that they name: `windows`: row t lists, in an order drawn for each row, tile t + dt for every dt in -1, 0, 1 with 0 <= t + dt < 16 and tile t + dt in the same clip as t, and -1 in all its other slots; clips are runs of whole consecutive temporal tiles.
All inputs are finite; a program needn't handle non-finite values.
Results may differ from a plain program's by a relative error of at most 0.012.
Values may be sent and summed in bfloat16 or wider, within the bound.
No kernel may reach another device: no remote copies, remote signals or barrier semaphores. Data moves between devices by JAX's collectives and lax.ppermute only.
A program may use at most 64 MiB of HBM per device.

v0:
```python
from functools import partial
import math
import jax
import jax.numpy as jnp
from jax import lax
from jax.sharding import PartitionSpec as P

HD = 128
SPATIAL = 1


def shifted(block, axis, distance):
    devices = range(lax.axis_size(axis))
    route = [(i - distance, i) for i in devices if i - distance in devices]
    return lax.ppermute(block, axis, route)


def from_behind(value, axis, steps):
    count = lax.axis_size(axis)
    pairs = [(source, (source + steps) % count) for source in range(count)]
    return lax.ppermute(value, axis, pairs)


def split_heads(slab, head_count):
    return slab.reshape(slab.shape[0], head_count, slab.shape[1] // head_count)


def tile_maxima(key_slab, head_count, spatial_count):
    parts = split_heads(key_slab, head_count).astype(jnp.float32)
    lengths = jnp.sqrt(jnp.sum(parts * parts, axis=2))
    return jnp.max(lengths.reshape(spatial_count, -1, head_count), axis=1)


def slab_keep(nearby, slab_tile, in_range, spatial_count, temporal_count):
    first = jnp.clip(slab_tile, 0, temporal_count - 1) * spatial_count
    return lax.dynamic_slice_in_dim(nearby, first, spatial_count, 1) & in_range


def attend(
    running,
    slab_entry,
    keep,
    query_parts,
    row_bound,
    head_count,
    spatial_count,
    tile_rows,
    score_scale,
):
    weighted, summed = running
    row_count = query_parts.shape[0]
    slab_keys = split_heads(slab_entry[0], head_count)
    slab_values = split_heads(slab_entry[1], head_count)
    scores = (
        jnp.einsum("qhd,khd->hqk", query_parts, slab_keys, preferred_element_type=jnp.float32)
        * score_scale
    )
    row_keep = jnp.broadcast_to(
        keep[:, None, :, None], (spatial_count, tile_rows, spatial_count, tile_rows)
    )
    row_keep = row_keep.reshape(row_count, row_count)
    weights = jnp.where(row_keep[None], jnp.exp(scores - row_bound.T[:, :, None]), 0.0)
    summed = summed + jnp.sum(weights, axis=2)
    weighted = weighted + jnp.einsum(
        "hqk,khd->qhd",
        weights.astype(jnp.bfloat16),
        slab_values,
        preferred_element_type=jnp.float32,
    )
    return (weighted, summed)


def on_device(query_heads, key_heads, value_heads, stream, out_weight, gate_scale, windows):
    queries = query_heads[0]
    own_keys = key_heads[0]
    own_values = value_heads[0]
    row_count, feature_count = queries.shape
    head_count = feature_count // HD
    spatial_count = SPATIAL
    tile_rows = row_count // spatial_count
    tile_count = windows.shape[0]
    temporal_count = tile_count // spatial_count
    score_scale = 1.0 / math.sqrt(HD)
    seq_count = lax.axis_size("seq")
    position = lax.axis_index("seq")
    temporal = position // 2
    allowed = jnp.any(
        windows[:, :, None] == jnp.arange(tile_count, dtype=jnp.int32)[None, None, :], axis=1
    )
    nearby = lax.dynamic_slice_in_dim(allowed, temporal * spatial_count, spatial_count, 0)
    always = jnp.array(True)
    slabs = [(own_keys, own_values, temporal, always)]
    reach = min(3, seq_count - 1)
    offsets = list(range(1, reach + 1)) + list(range(-reach, 0))
    for offset in offsets:
        moved_keys, moved_values = shifted((own_keys, own_values), "seq", offset)
        source = position - offset
        in_range = (source >= 0) & (source < seq_count)
        slabs.append((moved_keys, moved_values, source // 2, in_range))
    keeps = [
        slab_keep(nearby, slab_entry[2], slab_entry[3], spatial_count, temporal_count)
        for slab_entry in slabs
    ]
    bound_tiles = jnp.zeros((spatial_count, head_count), jnp.float32)
    for slab_entry, keep in zip(slabs, keeps):
        maxima = tile_maxima(slab_entry[0], head_count, spatial_count)
        candidate = jnp.where(keep[:, :, None], maxima[None, :, :], 0.0)
        bound_tiles = jnp.maximum(bound_tiles, jnp.max(candidate, axis=1))
    query_parts = split_heads(queries, head_count)
    query_float = query_parts.astype(jnp.float32)
    query_lengths = jnp.sqrt(jnp.sum(query_float * query_float, axis=2))
    row_bound = query_lengths * jnp.repeat(bound_tiles, tile_rows, axis=0) * score_scale
    running = (
        jnp.zeros((row_count, head_count, HD), jnp.float32),
        jnp.zeros((head_count, row_count), jnp.float32),
    )
    for slab_entry, keep in zip(slabs, keeps):
        step_fn = partial(
            attend,
            slab_entry=slab_entry,
            keep=keep,
            query_parts=query_parts,
            row_bound=row_bound,
            head_count=head_count,
            spatial_count=spatial_count,
            tile_rows=tile_rows,
            score_scale=score_scale,
        )
        running = step_fn(running)
    weighted, summed = running
    attended = (
        (weighted / summed.T[:, :, None]).astype(jnp.bfloat16).reshape(row_count, feature_count)
    )
    head_terms = jnp.dot(
        attended,
        lax.all_gather(out_weight[0], "seq", axis=1, tiled=True),
        preferred_element_type=jnp.float32,
    )
    mixed = lax.psum_scatter(
        head_terms.astype(jnp.bfloat16), "head", scatter_dimension=1, tiled=True
    ).astype(jnp.float32)
    updated = (stream[0].astype(jnp.float32) + gate_scale[0][None, :] * mixed).astype(jnp.bfloat16)
    handed = from_behind(updated, "section", 1)
    return handed[None]


def solution(mesh):
    in_specs = (
        P("section", "seq", "head"),
        P("section", "seq", "head"),
        P("section", "seq", "head"),
        P("section", "seq", "head"),
        P("section", "head", "seq"),
        P("section", "head"),
        P(),
    )
    out_specs = P("section", "seq", "head")
    return jax.shard_map(
        on_device, mesh=mesh, in_specs=in_specs, out_specs=out_specs, check_vma=False
    )
```

profile of v0, /device:TPU:2, one launch (start us, length us, event | category | flops | bytes accessed | tf_op | source)
XLA Modules:
  0.0 199.8 jit_solution(8086827323401507072)
XLA Ops:
  7.3 6.1 %collective-permute-start.4 = (bf16[192,768]{1,0:T(8,128)(2,1)}, bf16[192,768]{1,0:T(8,128)(2,1)S(1)}, u32[]{:S(2)}, u32[]{:S(2)}) collective-permute-start(bf16[192,768]{1,0:T(8,128)(2,1)} %bitcast.145), channel_id=1, source_target_pairs={{8,0},{12,4},{16,8},{20,12},{24,16},{28,20},{32,24},{36,28},{40,32... | collective-permute-start | bytes 884744 | tf_op jit(solution)/shard_map/ppermute | solution.py:15
  13.5 3.3 %collective-permute-start.5 = (bf16[192,768]{1,0:T(8,128)(2,1)}, bf16[192,768]{1,0:T(8,128)(2,1)S(1)}, u32[]{:S(2)}, u32[]{:S(2)}) collective-permute-start(bf16[192,768]{1,0:T(8,128)(2,1)} %bitcast.146), channel_id=1, source_target_pairs={{4,0},{8,4},{12,8},{16,12},{20,16},{24,20},{28,24},{32,28},{36,32}... | collective-permute-start | bytes 884744 | tf_op jit(solution)/shard_map/ppermute | solution.py:15
  16.7 1.9 collective-permute-start.2
  18.7 7.8 %collective-permute-start.3 = (bf16[192,768]{1,0:T(8,128)(2,1)}, bf16[192,768]{1,0:T(8,128)(2,1)}, u32[]{:S(2)}, u32[]{:S(2)}) collective-permute-start(bf16[192,768]{1,0:T(8,128)(2,1)} %bitcast.148), channel_id=1, source_target_pairs={{12,0},{16,4},{20,8},{24,12},{28,16},{32,20},{36,24},{40,28},{44,3... | collective-permute-start | bytes 884744 | tf_op jit(solution)/shard_map/ppermute | solution.py:15
  26.5 2.6 %collective-permute-start = (bf16[192,768]{1,0:T(8,128)(2,1)}, bf16[192,768]{1,0:T(8,128)(2,1)S(1)}, u32[]{:S(2)}, u32[]{:S(2)}) collective-permute-start(bf16[192,768]{1,0:T(8,128)(2,1)} %bitcast.149), channel_id=1, source_target_pairs={{0,4},{4,8},{8,12},{12,16},{16,20},{20,24},{24,28},{28,32},{32,36}... | collective-permute-start | bytes 884744 | tf_op jit(solution)/shard_map/ppermute | solution.py:15
  29.1 1.3 reshape_squeeze.11
  30.4 1.4 reshape_squeeze.10
  38.0 2.0 %collective-permute-start.1 = (bf16[192,768]{1,0:T(8,128)(2,1)S(1)}, bf16[192,768]{1,0:T(8,128)(2,1)}, u32[]{:S(2)}, u32[]{:S(2)}) collective-permute-start(bf16[192,768]{1,0:T(8,128)(2,1)S(1)} %bitcast.150), channel_id=1, source_target_pairs={{0,8},{4,12},{8,16},{12,20},{16,24},{20,28},{24,32},{28,36},{32,40... | collective-permute-start | bytes 884744 | tf_op jit(solution)/shard_map/ppermute | solution.py:15
  40.7 2.5 %collective-permute-start.6 = (bf16[192,768]{1,0:T(8,128)(2,1)S(1)}, bf16[192,768]{1,0:T(8,128)(2,1)}, u32[]{:S(2)}, u32[]{:S(2)}) collective-permute-start(bf16[192,768]{1,0:T(8,128)(2,1)S(1)} %bitcast.151), channel_id=1, source_target_pairs={{0,4},{4,8},{8,12},{12,16},{16,20},{20,24},{24,28},{28,32},{32,36}... | collective-permute-start | bytes 884744 | tf_op jit(solution)/shard_map/ppermute | solution.py:15
  43.8 6.9 %collective-permute-start.10 = (bf16[192,768]{1,0:T(8,128)(2,1)S(1)}, bf16[192,768]{1,0:T(8,128)(2,1)}, u32[]{:S(2)}, u32[]{:S(2)}) collective-permute-start(bf16[192,768]{1,0:T(8,128)(2,1)S(1)} %bitcast.152), channel_id=1, source_target_pairs={{8,0},{12,4},{16,8},{20,12},{24,16},{28,20},{32,24},{36,28},{40,32... | collective-permute-start | bytes 884744 | tf_op jit(solution)/shard_map/ppermute | solution.py:15
  51.7 4.7 %collective-permute-done.3 = bf16[192,768]{1,0:T(8,128)(2,1)} collective-permute-done((bf16[192,768]{1,0:T(8,128)(2,1)}, bf16[192,768]{1,0:T(8,128)(2,1)}, u32[]{:S(2)}, u32[]{:S(2)}) %collective-permute-start.3) | collective-permute-done | bytes 294944 | tf_op jit(solution)/shard_map/ppermute | solution.py:15
  56.4 7.9 %collective-permute-start.9 = (bf16[192,768]{1,0:T(8,128)(2,1)S(1)}, bf16[192,768]{1,0:T(8,128)(2,1)}, u32[]{:S(2)}, u32[]{:S(2)}) collective-permute-start(bf16[192,768]{1,0:T(8,128)(2,1)S(1)} %bitcast.153), channel_id=1, source_target_pairs={{12,0},{16,4},{20,8},{24,12},{28,16},{32,20},{36,24},{40,28},{44,3... | collective-permute-start | bytes 884744 | tf_op jit(solution)/shard_map/ppermute | solution.py:15
  64.3 1.3 reshape.183
  65.9 2.2 %collective-permute-start.8 = (bf16[192,768]{1,0:T(8,128)(2,1)S(1)}, bf16[192,768]{1,0:T(8,128)(2,1)S(1)}, u32[]{:S(2)}, u32[]{:S(2)}) collective-permute-start(bf16[192,768]{1,0:T(8,128)(2,1)S(1)} %bitcast.154), channel_id=1, source_target_pairs={{0,12},{4,16},{8,20},{12,24},{16,28},{20,32},{24,36},{28,40},{32,4... | collective-permute-start | bytes 884744 | tf_op jit(solution)/shard_map/ppermute | solution.py:15
  68.9 5.1 %collective-permute-start.11 = (bf16[192,768]{1,0:T(8,128)(2,1)S(1)}, bf16[192,768]{1,0:T(8,128)(2,1)}, u32[]{:S(2)}, u32[]{:S(2)}) collective-permute-start(bf16[192,768]{1,0:T(8,128)(2,1)S(1)} %bitcast.155), channel_id=1, source_target_pairs={{4,0},{8,4},{12,8},{16,12},{20,16},{24,20},{28,24},{32,28},{36,32}... | collective-permute-start | bytes 884744 | tf_op jit(solution)/shard_map/ppermute | solution.py:15
  74.0 1.3 reshape.181
  76.9 1.2 fusion.96
  78.9 1.4 fusion.93
  80.9 2.6 %collective-permute-start.7 = (bf16[192,768]{1,0:T(8,128)(2,1)S(1)}, bf16[192,768]{1,0:T(8,128)(2,1)S(1)}, u32[]{:S(2)}, u32[]{:S(2)}) collective-permute-start(bf16[192,768]{1,0:T(8,128)(2,1)S(1)} %bitcast.156), channel_id=1, source_target_pairs={{0,8},{4,12},{8,16},{12,20},{16,24},{20,28},{24,32},{28,36},{32,40... | collective-permute-start | bytes 884744 | tf_op jit(solution)/shard_map/ppermute | solution.py:15
  83.5 1.4 fusion.37
  84.9 3.7 %collective-permute-done.9 = bf16[192,768]{1,0:T(8,128)(2,1)} collective-permute-done((bf16[192,768]{1,0:T(8,128)(2,1)S(1)}, bf16[192,768]{1,0:T(8,128)(2,1)}, u32[]{:S(2)}, u32[]{:S(2)}) %collective-permute-start.9) | collective-permute-done | bytes 294944 | tf_op jit(solution)/shard_map/ppermute | solution.py:15
  88.6 1.4 fusion.39
  90.0 1.4 fusion.95
  91.9 2.7 %collective-permute-done.8 = bf16[192,768]{1,0:T(8,128)(2,1)S(1)} collective-permute-done((bf16[192,768]{1,0:T(8,128)(2,1)S(1)}, bf16[192,768]{1,0:T(8,128)(2,1)S(1)}, u32[]{:S(2)}, u32[]{:S(2)}) %collective-permute-start.8) | collective-permute-done | bytes 294944 | tf_op jit(solution)/shard_map/ppermute | solution.py:15
  95.2 1.4 fusion.35
  97.1 1.4 convolution_add_fusion.1
  98.4 2.4 %collective-permute-done.7 = bf16[192,768]{1,0:T(8,128)(2,1)S(1)} collective-permute-done((bf16[192,768]{1,0:T(8,128)(2,1)S(1)}, bf16[192,768]{1,0:T(8,128)(2,1)S(1)}, u32[]{:S(2)}, u32[]{:S(2)}) %collective-permute-start.7) | collective-permute-done | bytes 294944 | tf_op jit(solution)/shard_map/ppermute | solution.py:15
  101.3 31.5 %all-gather.3.cloned.1.call-done = bf16[1,768,3072]{1,2,0:T(8,128)(2,1)} async-done(((bf16[1,768,96]{1,2,0:T(8,128)(2,1)}), bf16[1,768,3072]{1,2,0:T(8,128)(2,1)}) %all-gather.3.cloned.1.call-update) | async-done | bytes 4718608 | tf_op jit(solution)/shard_map/all_gather | solution.py:136
  132.8 5.1 %fusion.2 = bf16[192,3072]{1,0:T(8,128)(2,1)} fusion(bf16[1,768,3072]{1,2,0:T(8,128)(2,1)} %all-gather.3.cloned.1.call-done, bf16[6,24,8,128]{3,2,1,0:T(8,128)(2,1)S(1)} %fusion.33), kind=kOutput, calls=%fused_computation.2 | convolution fusion | flops 906559488 | bytes 6193152 | tf_op jit(solution)/shard_map/dot_general | solution.py:134
  138.6 37.7 %reduce-scatter.2.cloned.1.call-done = bf16[192,768]{1,0:T(8,128)(2,1)} async-done(((bf16[192,3072]{1,0:T(8,128)(2,1)}), bf16[192,768]{1,0:T(8,128)(2,1)}) %reduce-scatter.2.cloned.1.call-update) | async-done | bytes 294928 | tf_op jit(solution)/shard_map/reduce_scatter | solution.py:139
  177.4 1.9 collective-permute-start.12
  179.3 13.0 %collective-permute-done.12 = bf16[192,768]{1,0:T(8,128)(2,1)S(1)} collective-permute-done((bf16[192,768]{1,0:T(8,128)(2,1)S(1)}, bf16[192,768]{1,0:T(8,128)(2,1)S(1)}, u32[]{:S(2)}, u32[]{:S(2)}) %collective-permute-start.12) | collective-permute-done | bytes 294944 | tf_op jit(solution)/shard_map/ppermute | solution.py:21
  (66 shorter events, 13.6 us)
Async XLA Ops:
  6.5 126.3 %all-gather.3.cloned.1.call-start = ((), (), s32[]{:S(2)}) async-start(), calls=%async_computation.2 | async-start | bytes 4866048 | tf_op jit(solution)/shard_map/all_gather | solution.py:136
  7.3 169.1 %reduce-scatter.2.cloned.1.call-start = ((), (), s32[]{:S(2)}) async-start(), calls=%async_computation.1 | async-start | bytes 1474560 | tf_op jit(solution)/shard_map/reduce_scatter | solution.py:139
  7.3 25.1 %copy-start.5 = (s32[16,27]{1,0:T(8,128)S(1)}, s32[16,27]{1,0:T(8,128)}, u32[]{:S(2)}) copy-start(s32[16,27]{1,0:T(8,128)} %param.13) | copy-start | bytes 5188
  7.3 30.7 %collective-permute-start.4 = (bf16[192,768]{1,0:T(8,128)(2,1)}, bf16[192,768]{1,0:T(8,128)(2,1)S(1)}, u32[]{:S(2)}, u32[]{:S(2)}) collective-permute-start(bf16[192,768]{1,0:T(8,128)(2,1)} %bitcast.145), channel_id=1, source_target_pairs={{8,0},{12,4},{16,8},{20,12},{24,16},{28,20},{32,24},{36,28},{40,32... | collective-permute-start | bytes 884744 | tf_op jit(solution)/shard_map/ppermute | solution.py:15
  13.5 27.2 %collective-permute-start.5 = (bf16[192,768]{1,0:T(8,128)(2,1)}, bf16[192,768]{1,0:T(8,128)(2,1)S(1)}, u32[]{:S(2)}, u32[]{:S(2)}) collective-permute-start(bf16[192,768]{1,0:T(8,128)(2,1)} %bitcast.146), channel_id=1, source_target_pairs={{4,0},{8,4},{12,8},{16,12},{20,16},{24,20},{28,24},{32,28},{36,32}... | collective-permute-start | bytes 884744 | tf_op jit(solution)/shard_map/ppermute | solution.py:15
  16.7 27.1 %collective-permute-start.2 = (bf16[192,768]{1,0:T(8,128)(2,1)}, bf16[192,768]{1,0:T(8,128)(2,1)S(1)}, u32[]{:S(2)}, u32[]{:S(2)}) collective-permute-start(bf16[192,768]{1,0:T(8,128)(2,1)} %bitcast.147), channel_id=1, source_target_pairs={{0,12},{4,16},{8,20},{12,24},{16,28},{20,32},{24,36},{28,40},{32,4... | collective-permute-start | bytes 884744 | tf_op jit(solution)/shard_map/ppermute | solution.py:15
  18.7 37.7 %collective-permute-start.3 = (bf16[192,768]{1,0:T(8,128)(2,1)}, bf16[192,768]{1,0:T(8,128)(2,1)}, u32[]{:S(2)}, u32[]{:S(2)}) collective-permute-start(bf16[192,768]{1,0:T(8,128)(2,1)} %bitcast.148), channel_id=1, source_target_pairs={{12,0},{16,4},{20,8},{24,12},{28,16},{32,20},{36,24},{40,28},{44,3... | collective-permute-start | bytes 884744 | tf_op jit(solution)/shard_map/ppermute | solution.py:15
  26.5 39.4 %collective-permute-start = (bf16[192,768]{1,0:T(8,128)(2,1)}, bf16[192,768]{1,0:T(8,128)(2,1)S(1)}, u32[]{:S(2)}, u32[]{:S(2)}) collective-permute-start(bf16[192,768]{1,0:T(8,128)(2,1)} %bitcast.149), channel_id=1, source_target_pairs={{0,4},{4,8},{8,12},{12,16},{16,20},{20,24},{24,28},{28,32},{32,36}... | collective-permute-start | bytes 884744 | tf_op jit(solution)/shard_map/ppermute | solution.py:15
  30.4 2.7 %copy-start.2 = (bf16[1,192,768]{2,1,0:T(8,128)(2,1)S(1)}, bf16[1,192,768]{2,1,0:T(8,128)(2,1)}, u32[]{:S(2)}) copy-start(bf16[1,192,768]{2,1,0:T(8,128)(2,1)} %param.9) | copy-start | bytes 884740
  31.8 6.2 %copy-start.1 = (bf16[1,192,768]{2,1,0:T(8,128)(2,1)S(1)}, bf16[1,192,768]{2,1,0:T(8,128)(2,1)}, u32[]{:S(2)}) copy-start(bf16[1,192,768]{2,1,0:T(8,128)(2,1)} %param.8) | copy-start | bytes 884740
  38.0 2.7 %copy-start.3 = (bf16[192,768]{1,0:T(8,128)(2,1)}, bf16[192,768]{1,0:T(8,128)(2,1)S(1)}, u32[]{:S(2)}) copy-start(bf16[192,768]{1,0:T(8,128)(2,1)S(1)} %collective-permute-done.4) | copy-start | bytes 884740
  38.0 30.9 %collective-permute-start.1 = (bf16[192,768]{1,0:T(8,128)(2,1)S(1)}, bf16[192,768]{1,0:T(8,128)(2,1)}, u32[]{:S(2)}, u32[]{:S(2)}) collective-permute-start(bf16[192,768]{1,0:T(8,128)(2,1)S(1)} %bitcast.150), channel_id=1, source_target_pairs={{0,8},{4,12},{8,16},{12,20},{16,24},{20,28},{24,32},{28,36},{32,40... | collective-permute-start | bytes 884744 | tf_op jit(solution)/shard_map/ppermute | solution.py:15
  40.7 56.4 %collective-permute-start.6 = (bf16[192,768]{1,0:T(8,128)(2,1)S(1)}, bf16[192,768]{1,0:T(8,128)(2,1)}, u32[]{:S(2)}, u32[]{:S(2)}) collective-permute-start(bf16[192,768]{1,0:T(8,128)(2,1)S(1)} %bitcast.151), channel_id=1, source_target_pairs={{0,4},{4,8},{8,12},{12,16},{16,20},{20,24},{24,28},{28,32},{32,36}... | collective-permute-start | bytes 884744 | tf_op jit(solution)/shard_map/ppermute | solution.py:15
  43.8 37.1 %collective-permute-start.10 = (bf16[192,768]{1,0:T(8,128)(2,1)S(1)}, bf16[192,768]{1,0:T(8,128)(2,1)}, u32[]{:S(2)}, u32[]{:S(2)}) collective-permute-start(bf16[192,768]{1,0:T(8,128)(2,1)S(1)} %bitcast.152), channel_id=1, source_target_pairs={{8,0},{12,4},{16,8},{20,12},{24,16},{28,20},{32,24},{36,28},{40,32... | collective-permute-start | bytes 884744 | tf_op jit(solution)/shard_map/ppermute | solution.py:15
  56.4 32.2 %collective-permute-start.9 = (bf16[192,768]{1,0:T(8,128)(2,1)S(1)}, bf16[192,768]{1,0:T(8,128)(2,1)}, u32[]{:S(2)}, u32[]{:S(2)}) collective-permute-start(bf16[192,768]{1,0:T(8,128)(2,1)S(1)} %bitcast.153), channel_id=1, source_target_pairs={{12,0},{16,4},{20,8},{24,12},{28,16},{32,20},{36,24},{40,28},{44,3... | collective-permute-start | bytes 884744 | tf_op jit(solution)/shard_map/ppermute | solution.py:15
  65.9 28.6 %collective-permute-start.8 = (bf16[192,768]{1,0:T(8,128)(2,1)S(1)}, bf16[192,768]{1,0:T(8,128)(2,1)S(1)}, u32[]{:S(2)}, u32[]{:S(2)}) collective-permute-start(bf16[192,768]{1,0:T(8,128)(2,1)S(1)} %bitcast.154), channel_id=1, source_target_pairs={{0,12},{4,16},{8,20},{12,24},{16,28},{20,32},{24,36},{28,40},{32,4... | collective-permute-start | bytes 884744 | tf_op jit(solution)/shard_map/ppermute | solution.py:15
  68.9 26.3 %collective-permute-start.11 = (bf16[192,768]{1,0:T(8,128)(2,1)S(1)}, bf16[192,768]{1,0:T(8,128)(2,1)}, u32[]{:S(2)}, u32[]{:S(2)}) collective-permute-start(bf16[192,768]{1,0:T(8,128)(2,1)S(1)} %bitcast.155), channel_id=1, source_target_pairs={{4,0},{8,4},{12,8},{16,12},{20,16},{24,20},{28,24},{32,28},{36,32}... | collective-permute-start | bytes 884744 | tf_op jit(solution)/shard_map/ppermute | solution.py:15
  76.9 1.2 copy-start.4
  80.9 20.0 %collective-permute-start.7 = (bf16[192,768]{1,0:T(8,128)(2,1)S(1)}, bf16[192,768]{1,0:T(8,128)(2,1)S(1)}, u32[]{:S(2)}, u32[]{:S(2)}) collective-permute-start(bf16[192,768]{1,0:T(8,128)(2,1)S(1)} %bitcast.156), channel_id=1, source_target_pairs={{0,8},{4,12},{8,16},{12,20},{16,24},{20,28},{24,32},{28,36},{32,40... | collective-permute-start | bytes 884744 | tf_op jit(solution)/shard_map/ppermute | solution.py:15
  137.9 0.7 copy-start.6
  137.9 38.4 %copy-start = (bf16[1,192,768]{2,1,0:T(8,128)(2,1)S(1)}, bf16[1,192,768]{2,1,0:T(8,128)(2,1)}, u32[]{:S(2)}) copy-start(bf16[1,192,768]{2,1,0:T(8,128)(2,1)} %param.10) | copy-start | bytes 884740
  177.4 14.9 %collective-permute-start.12 = (bf16[192,768]{1,0:T(8,128)(2,1)S(1)}, bf16[192,768]{1,0:T(8,128)(2,1)S(1)}, u32[]{:S(2)}, u32[]{:S(2)}) collective-permute-start(bf16[192,768]{1,0:T(8,128)(2,1)S(1)} %fusion.34), channel_id=1, source_target_pairs={{0,128},{128,256},{256,384},{384,0},{1,129},{129,257},{257,385},{3... | collective-permute-start | bytes 884744 | tf_op jit(solution)/shard_map/ppermute | solution.py:21
Sparse Core Ops, SparseCore 0:
  10.5 122.2 all-gather.2
  138.0 38.2 reduce-scatter.1
where the time goes:
time: 201 us; the launch traced here: 200 us
  waiting for transfers between devices  96.7 us (48%)
  starting transfers between devices  52.9 us (26%)
  matrix products  17.7 us (9%)
  between operations  17.7 us (9%)
  local copies, waits for them, and re-layouts  9.76 us (5%)
  other arithmetic  4.97 us (2%)
    ppermute x12, starting transfers between devices, shifted(): return lax.ppermute(block, axis, route)  51 us
    reduce_scatter x1, waiting for transfers between devices, on_device(): lax.psum_scatter(head_terms.astype(jnp.bfloat16), 'head', scatter_dimensi...  37.7 us
    all_gather x1, waiting for transfers between devices, on_device(): lax.all_gather(out_weight[0], 'seq', axis=1, tiled=True)  31.5 us
    ppermute x12, waiting for transfers between devices, shifted(): return lax.ppermute(block, axis, route)  13.8 us
    ppermute x1, waiting for transfers between devices, from_behind(): return lax.ppermute(value, axis, pairs)  13 us
    dot_general x7, matrix products, attend(): jnp.einsum('hqk,khd->qhd', weights.astype(jnp.bfloat16), slab_values, pre...  6.68 us
    dot_general x7, matrix products, attend(): jnp.einsum('qhd,khd->hqk', query_parts, slab_keys, preferred_element_type...  5.98 us
    dot_general x1, matrix products, on_device(): jnp.dot(attended, lax.all_gather(out_weight[0], 'seq', axis=1, tiled=True...  5.07 us
  transfers between devices with their start and end apart: 15, of which 8 were waited for; matrix products, arithmetic and copies ran while one was open for 12% of the time, Pallas kernels for 0%

commit v1 on v0

--- a/solution.py
+++ b/solution.py
@@ -7,6 +7,11 @@
 
 HD = 128
 SPATIAL = 1
+
+
+def gather_by_exchange(x, axis, dim):
+    copies = jnp.concatenate([x] * lax.axis_size(axis), axis=dim)
+    return lax.all_to_all(copies, axis, dim, dim, tiled=True)
 
 
 def shifted(block, axis, distance):
@@ -132,9 +137,7 @@
         (weighted / summed.T[:, :, None]).astype(jnp.bfloat16).reshape(row_count, feature_count)
     )
     head_terms = jnp.dot(
-        attended,
-        lax.all_gather(out_weight[0], "seq", axis=1, tiled=True),
-        preferred_element_type=jnp.float32,
+        attended, gather_by_exchange(out_weight[0], "seq", 1), preferred_element_type=jnp.float32
     )
     mixed = lax.psum_scatter(
         head_terms.astype(jnp.bfloat16), "head", scatter_dimension=1, tiled=True

time: 201 us -> 286 us (1.42)
  the two profiles are of different devices: /device:TPU:2 before, /device:TPU:6 now
where the time goes in v1:
time: 286 us; the launch traced here: 285 us
  waiting for transfers between devices  164 us (57%)
  starting transfers between devices  69.5 us (24%)
  matrix products  17.8 us (6%)
  between operations  17.7 us (6%)
  local copies, waits for them, and re-layouts  11.4 us (4%)
  other arithmetic  4.96 us (2%)
    ppermute x12, waiting for transfers between devices, shifted(): return lax.ppermute(block, axis, route)  108 us
    ppermute x12, starting transfers between devices, shifted(): return lax.ppermute(block, axis, route)  56.9 us
    reduce_scatter x1, waiting for transfers between devices, on_device(): lax.psum_scatter(head_terms.astype(jnp.bfloat16), 'head', scatter_dimensi...  42.4 us
    ppermute x1, waiting for transfers between devices, from_behind(): return lax.ppermute(value, axis, pairs)  13 us
    all_to_all x1, starting transfers between devices, gather_by_exchange(): return lax.all_to_all(copies, axis, dim, dim, tiled=True)  10.6 us
    dot_general x7, matrix products, attend(): jnp.einsum('hqk,khd->qhd', weights.astype(jnp.bfloat16), slab_values, pre...  6.71 us
    dot_general x7, matrix products, attend(): jnp.einsum('qhd,khd->hqk', query_parts, slab_keys, preferred_element_type...  5.99 us
  transfers between devices with their start and end apart: 15, of which 8 were waited for; matrix products, arithmetic and copies ran while one was open for 8% of the time, Pallas kernels for 0%

profile of v1, /device:TPU:6, one launch (start us, length us, event | category | flops | bytes accessed | tf_op | source)
XLA Modules:
  0.0 284.9 jit_solution(13911816502245838694)
XLA Ops:
  6.5 3.6 %concatenate.7 = bf16[768,32,96]{0,2,1:T(8,128)(2,1)} broadcast(bf16[768,96]{0,1:T(8,128)(2,1)} %bitcast.155), dimensions={0,2} | broadcast | bytes 4866048 | tf_op jit(solution)/shard_map/concatenate | solution.py:13
  10.2 10.6 %all-to-all-start = ((bf16[768,32,96]{0,2,1:T(8,128)(2,1)}), bf16[768,32,96]{0,2,1:T(8,128)(2,1)}, u32[]{:S(2)}, u32[]{:S(2)}) async-start(bf16[768,32,96]{0,2,1:T(8,128)(2,1)} %concatenate.7), calls=%async_computation | async-start | bytes 9437184 | tf_op jit(solution)/shard_map/all_to_all | solution.py:14
  20.8 4.9 %collective-permute-start.5 = (bf16[192,768]{1,0:T(8,128)(2,1)S(1)}, bf16[192,768]{1,0:T(8,128)(2,1)S(1)}, u32[]{:S(2)}, u32[]{:S(2)}) collective-permute-start(bf16[192,768]{1,0:T(8,128)(2,1)S(1)} %bitcast.143), channel_id=1, source_target_pairs={{4,0},{8,4},{12,8},{16,12},{20,16},{24,20},{28,24},{32,28},{36,32}... | collective-permute-start | bytes 884744 | tf_op jit(solution)/shard_map/ppermute | solution.py:20
  25.7 4.3 %collective-permute-start.4 = (bf16[192,768]{1,0:T(8,128)(2,1)S(1)}, bf16[192,768]{1,0:T(8,128)(2,1)}, u32[]{:S(2)}, u32[]{:S(2)}) collective-permute-start(bf16[192,768]{1,0:T(8,128)(2,1)S(1)} %bitcast.144), channel_id=1, source_target_pairs={{8,0},{12,4},{16,8},{20,12},{24,16},{28,20},{32,24},{36,28},{40,32... | collective-permute-start | bytes 884744 | tf_op jit(solution)/shard_map/ppermute | solution.py:20
  30.0 3.4 %collective-permute-start.3 = (bf16[192,768]{1,0:T(8,128)(2,1)S(1)}, bf16[192,768]{1,0:T(8,128)(2,1)S(1)}, u32[]{:S(2)}, u32[]{:S(2)}) collective-permute-start(bf16[192,768]{1,0:T(8,128)(2,1)S(1)} %bitcast.145), channel_id=1, source_target_pairs={{12,0},{16,4},{20,8},{24,12},{28,16},{32,20},{36,24},{40,28},{44,3... | collective-permute-start | bytes 884744 | tf_op jit(solution)/shard_map/ppermute | solution.py:20
  33.3 4.3 %collective-permute-start.2 = (bf16[192,768]{1,0:T(8,128)(2,1)S(1)}, bf16[192,768]{1,0:T(8,128)(2,1)S(1)}, u32[]{:S(2)}, u32[]{:S(2)}) collective-permute-start(bf16[192,768]{1,0:T(8,128)(2,1)S(1)} %bitcast.146), channel_id=1, source_target_pairs={{0,12},{4,16},{8,20},{12,24},{16,28},{20,32},{24,36},{28,40},{32,4... | collective-permute-start | bytes 884744 | tf_op jit(solution)/shard_map/ppermute | solution.py:20
  37.6 3.7 %collective-permute-start.1 = (bf16[192,768]{1,0:T(8,128)(2,1)S(1)}, bf16[192,768]{1,0:T(8,128)(2,1)S(1)}, u32[]{:S(2)}, u32[]{:S(2)}) collective-permute-start(bf16[192,768]{1,0:T(8,128)(2,1)S(1)} %bitcast.147), channel_id=1, source_target_pairs={{0,8},{4,12},{8,16},{12,20},{16,24},{20,28},{24,32},{28,36},{32,40... | collective-permute-start | bytes 884744 | tf_op jit(solution)/shard_map/ppermute | solution.py:20
  48.2 83.1 %collective-permute-done.5 = bf16[192,768]{1,0:T(8,128)(2,1)S(1)} collective-permute-done((bf16[192,768]{1,0:T(8,128)(2,1)S(1)}, bf16[192,768]{1,0:T(8,128)(2,1)S(1)}, u32[]{:S(2)}, u32[]{:S(2)}) %collective-permute-start.5) | collective-permute-done | bytes 294944 | tf_op jit(solution)/shard_map/ppermute | solution.py:20
  131.3 5.8 %collective-permute-start = (bf16[192,768]{1,0:T(8,128)(2,1)S(1)}, bf16[192,768]{1,0:T(8,128)(2,1)}, u32[]{:S(2)}, u32[]{:S(2)}) collective-permute-start(bf16[192,768]{1,0:T(8,128)(2,1)S(1)} %bitcast.148), channel_id=1, source_target_pairs={{0,4},{4,8},{8,12},{12,16},{16,20},{20,24},{24,28},{28,32},{32,36}... | collective-permute-start | bytes 884744 | tf_op jit(solution)/shard_map/ppermute | solution.py:20
  137.8 8.6 %collective-permute-done.4 = bf16[192,768]{1,0:T(8,128)(2,1)} collective-permute-done((bf16[192,768]{1,0:T(8,128)(2,1)S(1)}, bf16[192,768]{1,0:T(8,128)(2,1)}, u32[]{:S(2)}, u32[]{:S(2)}) %collective-permute-start.4) | collective-permute-done | bytes 294944 | tf_op jit(solution)/shard_map/ppermute | solution.py:20
  146.4 10.8 %collective-permute-start.11 = (bf16[192,768]{1,0:T(8,128)(2,1)S(1)}, bf16[192,768]{1,0:T(8,128)(2,1)}, u32[]{:S(2)}, u32[]{:S(2)}) collective-permute-start(bf16[192,768]{1,0:T(8,128)(2,1)S(1)} %bitcast.149), channel_id=1, source_target_pairs={{4,0},{8,4},{12,8},{16,12},{20,16},{24,20},{28,24},{32,28},{36,32}... | collective-permute-start | bytes 884744 | tf_op jit(solution)/shard_map/ppermute | solution.py:20
  157.3 1.3 reshape.252
  158.8 6.0 %collective-permute-done.3 = bf16[192,768]{1,0:T(8,128)(2,1)S(1)} collective-permute-done((bf16[192,768]{1,0:T(8,128)(2,1)S(1)}, bf16[192,768]{1,0:T(8,128)(2,1)S(1)}, u32[]{:S(2)}, u32[]{:S(2)}) %collective-permute-start.3) | collective-permute-done | bytes 294944 | tf_op jit(solution)/shard_map/ppermute | solution.py:20
  164.8 3.0 %collective-permute-start.10 = (bf16[192,768]{1,0:T(8,128)(2,1)S(1)}, bf16[192,768]{1,0:T(8,128)(2,1)}, u32[]{:S(2)}, u32[]{:S(2)}) collective-permute-start(bf16[192,768]{1,0:T(8,128)(2,1)S(1)} %bitcast.150), channel_id=1, source_target_pairs={{8,0},{12,4},{16,8},{20,12},{24,16},{28,20},{32,24},{36,28},{40,32... | collective-permute-start | bytes 884744 | tf_op jit(solution)/shard_map/ppermute | solution.py:20
  168.7 6.5 %collective-permute-start.9 = (bf16[192,768]{1,0:T(8,128)(2,1)S(1)}, bf16[192,768]{1,0:T(8,128)(2,1)}, u32[]{:S(2)}, u32[]{:S(2)}) collective-permute-start(bf16[192,768]{1,0:T(8,128)(2,1)S(1)} %bitcast.151), channel_id=1, source_target_pairs={{12,0},{16,4},{20,8},{24,12},{28,16},{32,20},{36,24},{40,28},{44,3... | collective-permute-start | bytes 884744 | tf_op jit(solution)/shard_map/ppermute | solution.py:20
  176.0 1.9 collective-permute-start.8
  178.6 1.9 collective-permute-start.6
  180.5 1.3 reshape.248
  183.4 1.1 fusion.91
  185.5 1.4 fusion.87
  187.5 6.5 %collective-permute-start.7 = (bf16[192,768]{1,0:T(8,128)(2,1)S(1)}, bf16[192,768]{1,0:T(8,128)(2,1)S(1)}, u32[]{:S(2)}, u32[]{:S(2)}) collective-permute-start(bf16[192,768]{1,0:T(8,128)(2,1)S(1)} %bitcast.154), channel_id=1, source_target_pairs={{0,8},{4,12},{8,16},{12,20},{16,24},{20,28},{24,32},{28,36},{32,40... | collective-permute-start | bytes 884744 | tf_op jit(solution)/shard_map/ppermute | solution.py:20
  193.9 1.4 fusion.30
  195.3 1.4 fusion.32
  197.1 1.4 fusion.92
  198.6 3.6 %collective-permute-done.9 = bf16[192,768]{1,0:T(8,128)(2,1)} collective-permute-done((bf16[192,768]{1,0:T(8,128)(2,1)S(1)}, bf16[192,768]{1,0:T(8,128)(2,1)}, u32[]{:S(2)}, u32[]{:S(2)}) %collective-permute-start.9) | collective-permute-done | bytes 294944 | tf_op jit(solution)/shard_map/ppermute | solution.py:20
  202.1 1.4 fusion.34
  203.5 1.4 fusion.36
  205.4 5.8 %collective-permute-done.6 = bf16[192,768]{1,0:T(8,128)(2,1)S(1)} collective-permute-done((bf16[192,768]{1,0:T(8,128)(2,1)S(1)}, bf16[192,768]{1,0:T(8,128)(2,1)S(1)}, u32[]{:S(2)}, u32[]{:S(2)}) %collective-permute-start.6) | collective-permute-done | bytes 294944 | tf_op jit(solution)/shard_map/ppermute | solution.py:20
  213.2 5.1 %convolution_convert_fusion = bf16[192,3072]{1,0:T(8,128)(2,1)} fusion(bf16[768,3072]{0,1:T(8,128)(2,1)} %bitcast.20, bf16[6,24,8,128]{3,2,1,0:T(8,128)(2,1)S(1)} %fusion.28), kind=kOutput, calls=%fused_computation | convolution fusion | flops 906559488 | bytes 6193152 | tf_op jit(solution)/shard_map/dot_general | solution.py:139
  218.9 42.4 %reduce-scatter.2.cloned.1.call-done = bf16[192,768]{1,0:T(8,128)(2,1)} async-done(((bf16[192,3072]{1,0:T(8,128)(2,1)}), bf16[192,768]{1,0:T(8,128)(2,1)}) %reduce-scatter.2.cloned.1.call-update) | async-done | bytes 294928 | tf_op jit(solution)/shard_map/reduce_scatter | solution.py:142
  262.4 1.9 collective-permute-start.12
  264.3 13.0 %collective-permute-done.12 = bf16[192,768]{1,0:T(8,128)(2,1)S(1)} collective-permute-done((bf16[192,768]{1,0:T(8,128)(2,1)S(1)}, bf16[192,768]{1,0:T(8,128)(2,1)S(1)}, u32[]{:S(2)}, u32[]{:S(2)}) %collective-permute-start.12) | collective-permute-done | bytes 294944 | tf_op jit(solution)/shard_map/ppermute | solution.py:26
  (68 shorter events, 14.5 us)
Async XLA Ops:
  10.1 10.6 %copy-start.2 = (bf16[1,192,768]{2,1,0:T(8,128)(2,1)S(1)}, bf16[1,192,768]{2,1,0:T(8,128)(2,1)}, u32[]{:S(2)}) copy-start(bf16[1,192,768]{2,1,0:T(8,128)(2,1)} %param.8) | copy-start | bytes 884740
  10.2 31.5 %copy-start.1 = (bf16[1,192,768]{2,1,0:T(8,128)(2,1)S(1)}, bf16[1,192,768]{2,1,0:T(8,128)(2,1)}, u32[]{:S(2)}) copy-start(bf16[1,192,768]{2,1,0:T(8,128)(2,1)} %param.7) | copy-start | bytes 884740
  10.2 203.0 %all-to-all-start = ((bf16[768,32,96]{0,2,1:T(8,128)(2,1)}), bf16[768,32,96]{0,2,1:T(8,128)(2,1)}, u32[]{:S(2)}, u32[]{:S(2)}) async-start(bf16[768,32,96]{0,2,1:T(8,128)(2,1)} %concatenate.7), calls=%async_computation | async-start | bytes 9437184 | tf_op jit(solution)/shard_map/all_to_all | solution.py:14
  20.7 240.6 %reduce-scatter.2.cloned.1.call-start = ((), (), s32[]{:S(2)}) async-start(), calls=%async_computation.2 | async-start | bytes 1474560 | tf_op jit(solution)/shard_map/reduce_scatter | solution.py:142
  20.8 21.8 %copy-start.6 = (s32[16,27]{1,0:T(8,128)S(1)}, s32[16,27]{1,0:T(8,128)}, u32[]{:S(2)}) copy-start(s32[16,27]{1,0:T(8,128)} %param.13) | copy-start | bytes 5188
  20.8 110.5 %collective-permute-start.5 = (bf16[192,768]{1,0:T(8,128)(2,1)S(1)}, bf16[192,768]{1,0:T(8,128)(2,1)S(1)}, u32[]{:S(2)}, u32[]{:S(2)}) collective-permute-start(bf16[192,768]{1,0:T(8,128)(2,1)S(1)} %bitcast.143), channel_id=1, source_target_pairs={{4,0},{8,4},{12,8},{16,12},{20,16},{24,20},{28,24},{32,28},{36,32}... | collective-permute-start | bytes 884744 | tf_op jit(solution)/shard_map/ppermute | solution.py:20
  25.7 120.7 %collective-permute-start.4 = (bf16[192,768]{1,0:T(8,128)(2,1)S(1)}, bf16[192,768]{1,0:T(8,128)(2,1)}, u32[]{:S(2)}, u32[]{:S(2)}) collective-permute-start(bf16[192,768]{1,0:T(8,128)(2,1)S(1)} %bitcast.144), channel_id=1, source_target_pairs={{8,0},{12,4},{16,8},{20,12},{24,16},{28,20},{32,24},{36,28},{40,32... | collective-permute-start | bytes 884744 | tf_op jit(solution)/shard_map/ppermute | solution.py:20
  30.0 134.9 %collective-permute-start.3 = (bf16[192,768]{1,0:T(8,128)(2,1)S(1)}, bf16[192,768]{1,0:T(8,128)(2,1)S(1)}, u32[]{:S(2)}, u32[]{:S(2)}) collective-permute-start(bf16[192,768]{1,0:T(8,128)(2,1)S(1)} %bitcast.145), channel_id=1, source_target_pairs={{12,0},{16,4},{20,8},{24,12},{28,16},{32,20},{36,24},{40,28},{44,3... | collective-permute-start | bytes 884744 | tf_op jit(solution)/shard_map/ppermute | solution.py:20
  33.3 135.4 %collective-permute-start.2 = (bf16[192,768]{1,0:T(8,128)(2,1)S(1)}, bf16[192,768]{1,0:T(8,128)(2,1)S(1)}, u32[]{:S(2)}, u32[]{:S(2)}) collective-permute-start(bf16[192,768]{1,0:T(8,128)(2,1)S(1)} %bitcast.146), channel_id=1, source_target_pairs={{0,12},{4,16},{8,20},{12,24},{16,28},{20,32},{24,36},{28,40},{32,4... | collective-permute-start | bytes 884744 | tf_op jit(solution)/shard_map/ppermute | solution.py:20
  37.6 138.3 %collective-permute-start.1 = (bf16[192,768]{1,0:T(8,128)(2,1)S(1)}, bf16[192,768]{1,0:T(8,128)(2,1)S(1)}, u32[]{:S(2)}, u32[]{:S(2)}) collective-permute-start(bf16[192,768]{1,0:T(8,128)(2,1)S(1)} %bitcast.147), channel_id=1, source_target_pairs={{0,8},{4,12},{8,16},{12,20},{16,24},{20,28},{24,32},{28,36},{32,40... | collective-permute-start | bytes 884744 | tf_op jit(solution)/shard_map/ppermute | solution.py:20
  41.7 1.7 copy-start.3
  131.3 15.1 %copy-start.4 = (bf16[192,768]{1,0:T(8,128)(2,1)}, bf16[192,768]{1,0:T(8,128)(2,1)S(1)}, u32[]{:S(2)}) copy-start(bf16[192,768]{1,0:T(8,128)(2,1)S(1)} %collective-permute-done.5) | copy-start | bytes 884740
  131.3 47.3 %collective-permute-start = (bf16[192,768]{1,0:T(8,128)(2,1)S(1)}, bf16[192,768]{1,0:T(8,128)(2,1)}, u32[]{:S(2)}, u32[]{:S(2)}) collective-permute-start(bf16[192,768]{1,0:T(8,128)(2,1)S(1)} %bitcast.148), channel_id=1, source_target_pairs={{0,4},{4,8},{8,12},{12,16},{16,20},{20,24},{24,28},{28,32},{32,36}... | collective-permute-start | bytes 884744 | tf_op jit(solution)/shard_map/ppermute | solution.py:20
  146.4 41.0 %collective-permute-start.11 = (bf16[192,768]{1,0:T(8,128)(2,1)S(1)}, bf16[192,768]{1,0:T(8,128)(2,1)}, u32[]{:S(2)}, u32[]{:S(2)}) collective-permute-start(bf16[192,768]{1,0:T(8,128)(2,1)S(1)} %bitcast.149), channel_id=1, source_target_pairs={{4,0},{8,4},{12,8},{16,12},{20,16},{24,20},{28,24},{32,28},{36,32}... | collective-permute-start | bytes 884744 | tf_op jit(solution)/shard_map/ppermute | solution.py:20
  164.8 30.5 %collective-permute-start.10 = (bf16[192,768]{1,0:T(8,128)(2,1)S(1)}, bf16[192,768]{1,0:T(8,128)(2,1)}, u32[]{:S(2)}, u32[]{:S(2)}) collective-permute-start(bf16[192,768]{1,0:T(8,128)(2,1)S(1)} %bitcast.150), channel_id=1, source_target_pairs={{8,0},{12,4},{16,8},{20,12},{24,16},{28,20},{32,24},{36,28},{40,32... | collective-permute-start | bytes 884744 | tf_op jit(solution)/shard_map/ppermute | solution.py:20
  168.7 33.4 %collective-permute-start.9 = (bf16[192,768]{1,0:T(8,128)(2,1)S(1)}, bf16[192,768]{1,0:T(8,128)(2,1)}, u32[]{:S(2)}, u32[]{:S(2)}) collective-permute-start(bf16[192,768]{1,0:T(8,128)(2,1)S(1)} %bitcast.151), channel_id=1, source_target_pairs={{12,0},{16,4},{20,8},{24,12},{28,16},{32,20},{36,24},{40,28},{44,3... | collective-permute-start | bytes 884744 | tf_op jit(solution)/shard_map/ppermute | solution.py:20
  176.0 27.5 %collective-permute-start.8 = (bf16[192,768]{1,0:T(8,128)(2,1)S(1)}, bf16[192,768]{1,0:T(8,128)(2,1)}, u32[]{:S(2)}, u32[]{:S(2)}) collective-permute-start(bf16[192,768]{1,0:T(8,128)(2,1)S(1)} %bitcast.152), channel_id=1, source_target_pairs={{0,12},{4,16},{8,20},{12,24},{16,28},{20,32},{24,36},{28,40},{32,4... | collective-permute-start | bytes 884744 | tf_op jit(solution)/shard_map/ppermute | solution.py:20
  178.6 32.6 %collective-permute-start.6 = (bf16[192,768]{1,0:T(8,128)(2,1)S(1)}, bf16[192,768]{1,0:T(8,128)(2,1)S(1)}, u32[]{:S(2)}, u32[]{:S(2)}) collective-permute-start(bf16[192,768]{1,0:T(8,128)(2,1)S(1)} %bitcast.153), channel_id=1, source_target_pairs={{0,4},{4,8},{8,12},{12,16},{16,20},{20,24},{24,28},{28,32},{32,36}... | collective-permute-start | bytes 884744 | tf_op jit(solution)/shard_map/ppermute | solution.py:20
  183.4 1.2 copy-start.5
  187.5 25.2 %collective-permute-start.7 = (bf16[192,768]{1,0:T(8,128)(2,1)S(1)}, bf16[192,768]{1,0:T(8,128)(2,1)S(1)}, u32[]{:S(2)}, u32[]{:S(2)}) collective-permute-start(bf16[192,768]{1,0:T(8,128)(2,1)S(1)} %bitcast.154), channel_id=1, source_target_pairs={{0,8},{4,12},{8,16},{12,20},{16,24},{20,28},{24,32},{28,36},{32,40... | collective-permute-start | bytes 884744 | tf_op jit(solution)/shard_map/ppermute | solution.py:20
  218.2 0.7 copy-start.7
  218.2 43.1 %copy-start = (bf16[1,192,768]{2,1,0:T(8,128)(2,1)S(1)}, bf16[1,192,768]{2,1,0:T(8,128)(2,1)}, u32[]{:S(2)}) copy-start(bf16[1,192,768]{2,1,0:T(8,128)(2,1)} %param.10) | copy-start | bytes 884740
  262.4 14.9 %collective-permute-start.12 = (bf16[192,768]{1,0:T(8,128)(2,1)S(1)}, bf16[192,768]{1,0:T(8,128)(2,1)S(1)}, u32[]{:S(2)}, u32[]{:S(2)}) collective-permute-start(bf16[192,768]{1,0:T(8,128)(2,1)S(1)} %fusion.29), channel_id=1, source_target_pairs={{0,128},{128,256},{256,384},{384,0},{1,129},{129,257},{257,385},{3... | collective-permute-start | bytes 884744 | tf_op jit(solution)/shard_map/ppermute | solution.py:26
Sparse Core Ops, SparseCore 0:
  218.4 42.9 reduce-scatter.1
